TPU v7x, 512 devices: a whole 4x4x16 slice. The times are simulated.
512 devices in a mesh: seq: 64 (over z, x_hi, core), section: 8 (over y, x_lo).
Axes of the slice: x: 4 (x_hi: 2, x_lo: 2; x = x_hi * 2 + x_lo), y: 4, z: 16, core: 2. Of those that a mesh axis runs over, the one named last changes fastest.
Arguments:
- fwd_input: bfloat16 [8, 16384, 768], P('section', 'seq'), may hold values from -6 to 6
- bwd_input: bfloat16 [8, 16384, 768], P('section', 'seq'), may hold values from -6 to 6
- bwd_cotangent: bfloat16 [8, 16384, 768], P('section', 'seq'), may hold values from -6 to 6
- conv_weight: bfloat16 [8, 2, 3, 768, 384], P('section', None, None, 'seq'), may hold values from -0.125 to 0.125
- proj_weight: bfloat16 [8, 2, 384, 768], P('section', None, 'seq'), may hold values from -0.3125 to 0.3125
Outputs:
- next_input: bfloat16 [8, 16384, 768], P('section', 'seq')
- prev_cotangent: bfloat16 [8, 16384, 768], P('section', 'seq')
All inputs are finite; a program needn't handle non-finite values.
Results may differ from a plain program's by a relative error of at most 0.012.
Values may be sent and summed in bfloat16 or wider, within the bound.
No kernel may reach another device: no remote copies, remote signals or barrier semaphores. Data moves between devices by JAX's collectives and lax.ppermute only.
A program may use at most 64 MiB of HBM per device.

v0:
```python
import jax
import jax.numpy as jnp
from jax import lax
from jax.sharding import PartitionSpec as P

BLOCKS = 2
FIRST_DILATION = 128


def padded(x, sides, width):
    for axis, dim in sides:
        size, length = (lax.axis_size(axis), x.shape[dim])
        up = [(i, (i + 1) % size) for i in range(size - 1)]
        down = [(j, i) for i, j in up]
        last = lax.slice_in_dim(x, length - width, length, axis=dim)
        initial = lax.slice_in_dim(x, 0, width, axis=dim)
        before = lax.ppermute(last, axis, up)
        after = lax.ppermute(initial, axis, down)
        x = jnp.concatenate([before, x, after], axis=dim)
    return x


def from_behind(block, axis, distance):
    devices = range(lax.axis_size(axis))
    route = [(i - distance, i) for i in devices if i - distance in devices]
    return lax.ppermute(block, axis, route)


def from_behind_2(block, axis, distance):
    devices = range(lax.axis_size(axis))
    route = [((i - distance) % len(devices), i) for i in devices]
    return lax.ppermute(block, axis, route)


def gelu_back(value, cotangent):
    return jax.vjp(jax.nn.gelu, value)[1](cotangent)[0]


def rounded(product):
    return lax.optimization_barrier(product.astype(jnp.bfloat16)).astype(jnp.float32)


def reach(values, spacing_gap):
    length = values.shape[1]
    if spacing_gap < length:
        padded_input = padded(values, (("seq", 1),), spacing_gap)
        return (padded_input[:, :length], padded_input[:, 2 * spacing_gap :])
    shard_hops = spacing_gap // length
    earlier = from_behind(values, "seq", shard_hops)
    later = from_behind(values, "seq", -shard_hops)
    return (earlier, later)


def conv_apply(values, weight):
    return jnp.einsum("krc,ch->krh", values, weight, preferred_element_type=jnp.float32)


def conv_transpose(values, weight):
    return jnp.einsum("krh,ch->krc", values, weight, preferred_element_type=jnp.float32)


def run_forward(present_state, pieces):
    stored = []
    for depth_level in range(BLOCKS):
        conv_part, proj_part = pieces[depth_level]
        spacing_gap = FIRST_DILATION * 4**depth_level
        activated = jax.nn.gelu(present_state.astype(jnp.float32)).astype(jnp.bfloat16)
        middle = conv_apply(activated, conv_part[1])
        earlier, later = reach(activated, spacing_gap)
        preact = (
            rounded(conv_apply(earlier, conv_part[0]))
            + middle
            + rounded(conv_apply(later, conv_part[2]))
        )
        hidden = jax.nn.gelu(preact).astype(jnp.bfloat16)
        stored.append((present_state, preact))
        branch = jnp.einsum("krh,hc->krc", hidden, proj_part, preferred_element_type=jnp.float32)
        present_state = (present_state.astype(jnp.float32) + branch).astype(jnp.bfloat16)
    return (present_state, stored)


def local(fwd_input, bwd_input, bwd_cotangent, conv_weight, proj_weight):
    convolution_complete, proj_full = (
        lax.all_gather(conv_weight, "seq", axis=3, tiled=True),
        lax.all_gather(proj_weight, "seq", axis=2, tiled=True),
    )
    pieces = [
        (convolution_complete[0, depth_level], proj_full[0, depth_level])
        for depth_level in range(BLOCKS)
    ]
    forward_out, unused = run_forward(fwd_input, pieces)
    unused_out, stored = run_forward(bwd_input, pieces)
    cotangent = bwd_cotangent
    for depth_level in reversed(range(BLOCKS)):
        conv_part, proj_part = pieces[depth_level]
        spacing_gap = FIRST_DILATION * 4**depth_level
        block_in, preact = stored[depth_level]
        d_hidden = jnp.einsum(
            "krc,hc->krh", cotangent, proj_part, preferred_element_type=jnp.float32
        )
        d_preact = gelu_back(preact, d_hidden).astype(jnp.bfloat16)
        earlier, later = reach(d_preact, spacing_gap)
        d_act = (
            conv_transpose(later, conv_part[0])
            + conv_transpose(d_preact, conv_part[1])
            + conv_transpose(earlier, conv_part[2])
        )
        total = cotangent.astype(jnp.float32) + gelu_back(block_in.astype(jnp.float32), d_act)
        cotangent = total.astype(jnp.bfloat16)
    next_input = from_behind_2(forward_out, "section", 1)
    prev_cotangent = from_behind_2(cotangent, "section", -1)
    return (next_input, prev_cotangent)


def solution(mesh):
    in_specs = (
        P("section", "seq", None),
        P("section", "seq", None),
        P("section", "seq", None),
        P("section", None, None, "seq", None),
        P("section", None, "seq", None),
    )
    out_specs = (P("section", "seq", None), P("section", "seq", None))
    return jax.shard_map(local, mesh=mesh, in_specs=in_specs, out_specs=out_specs, check_vma=False)
```

profile of v0, /device:TPU:103, one launch (start us, length us, event | category | flops | bytes accessed | tf_op | source)
XLA Modules:
  0.0 411.6 jit_solution(7806383991603172441)
XLA Ops:
  11.6 6.1 %collective-permute-start.5 = (bf16[1,128,768]{2,1,0:T(8,128)(2,1)}, bf16[1,128,768]{2,1,0:T(8,128)(2,1)}, u32[]{:S(2)}, u32[]{:S(2)}) collective-permute-start(bf16[1,128,768]{2,1,0:T(8,128)(2,1)} %get-tuple-element.10), channel_id=1, source_target_pairs={{0,8},{8,16},{16,24},{24,32},{32,40},{40,48},{48,56},{56,64},{64,7... | collective-permute-start | bytes 589832 | tf_op jit(solution)/shard_map/ppermute | solution.py:17
  17.7 1.9 collective-permute-start.6
  21.5 7.2 %collective-permute-start = (bf16[1,128,768]{2,1,0:T(8,128)(2,1)}, bf16[1,128,768]{2,1,0:T(8,128)(2,1)}, u32[]{:S(2)}, u32[]{:S(2)}) collective-permute-start(bf16[1,128,768]{2,1,0:T(8,128)(2,1)} %get-tuple-element.12), channel_id=1, source_target_pairs={{0,8},{8,16},{16,24},{24,32},{32,40},{40,48},{48,56},{56,64},{64,7... | collective-permute-start | bytes 589832 | tf_op jit(solution)/shard_map/ppermute | solution.py:17
  28.8 1.9 collective-permute-start.1
  30.7 123.7 %all-gather.5.cloned.1.call-done = bf16[1,2,384,768]{3,1,0,2:T(2,128)(2,1)} async-done(((bf16[1,2,6,768]{3,1,0,2:T(2,128)(2,1)}), bf16[1,2,384,768]{3,1,0,2:T(2,128)(2,1)}) %all-gather.5.cloned.1.call-update) | async-done | bytes 1179664 | tf_op jit(solution)/shard_map/all_gather | solution.py:85
  154.4 5.1 %fusion.172 = (bf16[1,1,384,768]{3,1,0,2:T(2,128)(2,1)}, bf16[1,1,384,768]{3,1,0,2:T(2,128)(2,1)}) fusion(bf16[1,2,384,768]{3,1,0,2:T(2,128)(2,1)} %all-gather.5.cloned.1.call-done), kind=kLoop, calls=%fused_computation.215 | loop fusion | bytes 2359296 | tf_op jit(solution)/shard_map/slice | solution.py:88
  159.5 141.4 %all-gather.3.cloned.1.call-done = bf16[1,2,3,768,384]{4,1,2,0,3:T(2,128)(2,1)} async-done(((bf16[1,2,3,12,384]{4,1,2,0,3:T(2,128)(2,1)}), bf16[1,2,3,768,384]{4,1,2,0,3:T(2,128)(2,1)}) %all-gather.3.cloned.1.call-update) | async-done | bytes 3538960 | tf_op jit(solution)/shard_map/all_gather | solution.py:84
  300.9 9.0 %fusion.171 = (bf16[1,1,1,768,384]{4,1,2,0,3:T(2,128)(2,1)}, bf16[1,1,1,768,384]{4,1,2,0,3:T(2,128)(2,1)}, bf16[1,1,1,768,384]{4,1,2,0,3:T(2,128)(2,1)S(1)}, bf1...) fusion(bf16[1,2,3,768,384]{4,1,2,0,3:T(2,128)(2,1)} %all-gather, ...), kind=kLoop, calls=%fused_computation.214 | loop fusion | bytes 7077888 | tf_op jit(solution)/shard_map/slice | solution.py:68
  315.6 3.8 collective-permute-start.7
  319.4 3.0 collective-permute-start.8
  322.4 2.0 fusion.15
  324.4 2.0 fusion.16
  326.4 3.5 fusion.44
  329.9 5.9 %collective-permute-start.2 = (bf16[1,256,768]{2,1,0:T(8,128)(2,1)}, bf16[1,256,768]{2,1,0:T(8,128)(2,1)S(1)}, u32[]{:S(2)}, u32[]{:S(2)}) collective-permute-start(bf16[1,256,768]{2,1,0:T(8,128)(2,1)} %get-tuple-element.16), channel_id=1, source_target_pairs={{0,16},{8,24},{16,32},{24,40},{32,48},{40,56},{48,64},{56,72},{64,... | collective-permute-start | bytes 1179656 | tf_op jit(solution)/shard_map/ppermute | solution.py:26
  340.0 6.2 %collective-permute-done.8 = bf16[1,256,768]{2,1,0:T(8,128)(2,1)} collective-permute-done((bf16[1,256,768]{2,1,0:T(8,128)(2,1)}, bf16[1,256,768]{2,1,0:T(8,128)(2,1)}, u32[]{:S(2)}, u32[]{:S(2)}) %collective-permute-start.8) | collective-permute-done | bytes 393248 | tf_op jit(solution)/shard_map/ppermute | solution.py:26
  350.1 6.9 %collective-permute-start.10 = (bf16[1,256,384]{2,1,0:T(8,128)(2,1)}, bf16[1,256,384]{2,1,0:T(8,128)(2,1)}, u32[]{:S(2)}, u32[]{:S(2)}) collective-permute-start(bf16[1,256,384]{2,1,0:T(8,128)(2,1)} %fusion.70), channel_id=1, source_target_pairs={{0,16},{8,24},{16,32},{24,40},{32,48},{40,56},{48,64},{56,72},{64,... | collective-permute-start | bytes 589832 | tf_op jit(solution)/shard_map/ppermute | solution.py:26
  357.0 2.1 collective-permute-start.9
  361.3 3.5 fusion.5
  364.8 3.4 collective-permute-start.4
  374.0 8.8 %collective-permute-start.12 = (bf16[1,128,384]{2,1,0:T(8,128)(2,1)S(1)}, bf16[1,128,384]{2,1,0:T(8,128)(2,1)S(1)}, u32[]{:S(2)}, u32[]{:S(2)}) collective-permute-start(bf16[1,128,384]{2,1,0:T(8,128)(2,1)S(1)} %get-tuple-element.15), channel_id=1, source_target_pairs={{0,8},{8,16},{16,24},{24,32},{32,40},{40,48},{48,56},{56,64},{64,7... | collective-permute-start | bytes 294920 | tf_op jit(solution)/shard_map/ppermute | solution.py:17
  383.3 2.1 collective-permute-start.11
  385.7 7.3 %collective-permute-done.11 = bf16[1,128,384]{2,1,0:T(8,128)(2,1)S(1)} collective-permute-done((bf16[1,128,384]{2,1,0:T(8,128)(2,1)S(1)}, bf16[1,128,384]{2,1,0:T(8,128)(2,1)S(1)}, u32[]{:S(2)}, u32[]{:S(2)}) %collective-permute-start.11) | collective-permute-done | bytes 98336 | tf_op jit(solution)/shard_map/ppermute | solution.py:18
  393.9 1.9 collective-permute-start.13
  395.8 7.5 %collective-permute-done.13 = bf16[1,256,768]{2,1,0:T(8,128)(2,1)S(1)} collective-permute-done((bf16[1,256,768]{2,1,0:T(8,128)(2,1)S(1)}, bf16[1,256,768]{2,1,0:T(8,128)(2,1)S(1)}, u32[]{:S(2)}, u32[]{:S(2)}) %collective-permute-start.13) | collective-permute-done | bytes 393248 | tf_op jit(solution)/shard_map/ppermute | solution.py:32
  (83 shorter events, 30.7 us)
Async XLA Ops:
  7.2 12.5 %copy-start.12 = (bf16[1,256,768]{2,1,0:T(8,128)(2,1)S(1)}, bf16[1,256,768]{2,1,0:T(8,128)(2,1)}, u32[]{:S(2)}) copy-start(bf16[1,256,768]{2,1,0:T(8,128)(2,1)} %param.5) | copy-start | bytes 1179652
  7.2 147.3 %all-gather.5.cloned.1.call-start = ((), (), s32[]{:S(2)}) async-start(), calls=%async_computation.1 | async-start | bytes 1198080 | tf_op jit(solution)/shard_map/all_gather | solution.py:85
  7.9 293.0 %all-gather.3.cloned.1.call-start = ((), (), s32[]{:S(2)}) async-start(), calls=%async_computation | async-start | bytes 3594240 | tf_op jit(solution)/shard_map/all_gather | solution.py:84
  11.6 298.4 %collective-permute-start.5 = (bf16[1,128,768]{2,1,0:T(8,128)(2,1)}, bf16[1,128,768]{2,1,0:T(8,128)(2,1)}, u32[]{:S(2)}, u32[]{:S(2)}) collective-permute-start(bf16[1,128,768]{2,1,0:T(8,128)(2,1)} %get-tuple-element.10), channel_id=1, source_target_pairs={{0,8},{8,16},{16,24},{24,32},{32,40},{40,48},{48,56},{56,64},{64,7... | collective-permute-start | bytes 589832 | tf_op jit(solution)/shard_map/ppermute | solution.py:17
  17.7 293.8 %collective-permute-start.6 = (bf16[1,128,768]{2,1,0:T(8,128)(2,1)}, bf16[1,128,768]{2,1,0:T(8,128)(2,1)}, u32[]{:S(2)}, u32[]{:S(2)}) collective-permute-start(bf16[1,128,768]{2,1,0:T(8,128)(2,1)} %get-tuple-element.11), channel_id=1, source_target_pairs={{8,0},{16,8},{24,16},{32,24},{40,32},{48,40},{56,48},{64,56},{72,6... | collective-permute-start | bytes 589832 | tf_op jit(solution)/shard_map/ppermute | solution.py:18
  21.5 300.9 %collective-permute-start = (bf16[1,128,768]{2,1,0:T(8,128)(2,1)}, bf16[1,128,768]{2,1,0:T(8,128)(2,1)}, u32[]{:S(2)}, u32[]{:S(2)}) collective-permute-start(bf16[1,128,768]{2,1,0:T(8,128)(2,1)} %get-tuple-element.12), channel_id=1, source_target_pairs={{0,8},{8,16},{16,24},{24,32},{32,40},{40,48},{48,56},{56,64},{64,7... | collective-permute-start | bytes 589832 | tf_op jit(solution)/shard_map/ppermute | solution.py:17
  28.8 295.7 %collective-permute-start.1 = (bf16[1,128,768]{2,1,0:T(8,128)(2,1)}, bf16[1,128,768]{2,1,0:T(8,128)(2,1)}, u32[]{:S(2)}, u32[]{:S(2)}) collective-permute-start(bf16[1,128,768]{2,1,0:T(8,128)(2,1)} %get-tuple-element.13), channel_id=1, source_target_pairs={{8,0},{16,8},{24,16},{32,24},{40,32},{48,40},{56,48},{64,56},{72,6... | collective-permute-start | bytes 589832 | tf_op jit(solution)/shard_map/ppermute | solution.py:18
  300.9 9.0 %copy-start.4 = (bf16[1,256,768]{2,1,0:T(8,128)(2,1)S(1)}, bf16[1,256,768]{2,1,0:T(8,128)(2,1)}, u32[]{:S(2)}) copy-start(bf16[1,256,768]{2,1,0:T(8,128)(2,1)} %copy-done.3) | copy-start | bytes 1179652
  310.0 12.5 %copy-start.5 = (bf16[1,1,1,768,384]{4,1,2,0,3:T(2,128)(2,1)}, bf16[1,1,1,768,384]{4,1,2,0,3:T(2,128)(2,1)S(1)}, u32[]{:S(2)}) copy-start(bf16[1,1,1,768,384]{4,1,2,0,3:T(2,128)(2,1)S(1)} %get-tuple-element.6) | copy-start | bytes 1769476
  315.6 22.5 %collective-permute-start.7 = (bf16[1,256,768]{2,1,0:T(8,128)(2,1)}, bf16[1,256,768]{2,1,0:T(8,128)(2,1)}, u32[]{:S(2)}, u32[]{:S(2)}) collective-permute-start(bf16[1,256,768]{2,1,0:T(8,128)(2,1)} %get-tuple-element.18), channel_id=1, source_target_pairs={{0,16},{8,24},{16,32},{24,40},{32,48},{40,56},{48,64},{56,72},{64,... | collective-permute-start | bytes 1179656 | tf_op jit(solution)/shard_map/ppermute | solution.py:26
  319.4 26.8 %collective-permute-start.8 = (bf16[1,256,768]{2,1,0:T(8,128)(2,1)}, bf16[1,256,768]{2,1,0:T(8,128)(2,1)}, u32[]{:S(2)}, u32[]{:S(2)}) collective-permute-start(bf16[1,256,768]{2,1,0:T(8,128)(2,1)} %get-tuple-element.18), channel_id=1, source_target_pairs={{16,0},{24,8},{32,16},{40,24},{48,32},{56,40},{64,48},{72,56},{80,... | collective-permute-start | bytes 1179656 | tf_op jit(solution)/shard_map/ppermute | solution.py:26
  329.9 29.2 %collective-permute-start.2 = (bf16[1,256,768]{2,1,0:T(8,128)(2,1)}, bf16[1,256,768]{2,1,0:T(8,128)(2,1)S(1)}, u32[]{:S(2)}, u32[]{:S(2)}) collective-permute-start(bf16[1,256,768]{2,1,0:T(8,128)(2,1)} %get-tuple-element.16), channel_id=1, source_target_pairs={{0,16},{8,24},{16,32},{24,40},{32,48},{40,56},{48,64},{56,72},{64,... | collective-permute-start | bytes 1179656 | tf_op jit(solution)/shard_map/ppermute | solution.py:26
  335.8 24.4 %collective-permute-start.3 = (bf16[1,256,768]{2,1,0:T(8,128)(2,1)}, bf16[1,256,768]{2,1,0:T(8,128)(2,1)S(1)}, u32[]{:S(2)}, u32[]{:S(2)}) collective-permute-start(bf16[1,256,768]{2,1,0:T(8,128)(2,1)} %get-tuple-element.16), channel_id=1, source_target_pairs={{16,0},{24,8},{32,16},{40,24},{48,32},{56,40},{64,48},{72,56},{80,... | collective-permute-start | bytes 1179656 | tf_op jit(solution)/shard_map/ppermute | solution.py:26
  338.1 9.4 %copy-start = (bf16[1,1,1,768,384]{4,1,2,0,3:T(2,128)(2,1)S(1)}, bf16[1,1,1,768,384]{4,1,2,0,3:T(2,128)(2,1)}, u32[]{:S(2)}) copy-start(bf16[1,1,1,768,384]{4,1,2,0,3:T(2,128)(2,1)} %get-tuple-element.2) | copy-start | bytes 1769476
  338.1 9.4 %copy-start.19 = (bf16[1,256,768]{2,1,0:T(8,128)(2,1)S(1)}, bf16[1,256,768]{2,1,0:T(8,128)(2,1)}, u32[]{:S(2)}) copy-start(bf16[1,256,768]{2,1,0:T(8,128)(2,1)} %get-tuple-element.19) | copy-start | bytes 1179652
  348.9 10.2 %copy-start.7 = (bf16[1,1,1,768,384]{4,1,2,0,3:T(2,128)(2,1)S(1)}, bf16[1,1,1,768,384]{4,1,2,0,3:T(2,128)(2,1)}, u32[]{:S(2)}) copy-start(bf16[1,1,1,768,384]{4,1,2,0,3:T(2,128)(2,1)} %get-tuple-element.3) | copy-start | bytes 1769476
  350.1 19.9 %collective-permute-start.10 = (bf16[1,256,384]{2,1,0:T(8,128)(2,1)}, bf16[1,256,384]{2,1,0:T(8,128)(2,1)}, u32[]{:S(2)}, u32[]{:S(2)}) collective-permute-start(bf16[1,256,384]{2,1,0:T(8,128)(2,1)} %fusion.70), channel_id=1, source_target_pairs={{0,16},{8,24},{16,32},{24,40},{32,48},{40,56},{48,64},{56,72},{64,... | collective-permute-start | bytes 589832 | tf_op jit(solution)/shard_map/ppermute | solution.py:26
  357.0 14.5 %collective-permute-start.9 = (bf16[1,256,384]{2,1,0:T(8,128)(2,1)}, bf16[1,256,384]{2,1,0:T(8,128)(2,1)}, u32[]{:S(2)}, u32[]{:S(2)}) collective-permute-start(bf16[1,256,384]{2,1,0:T(8,128)(2,1)} %fusion.70), channel_id=1, source_target_pairs={{16,0},{24,8},{32,16},{40,24},{48,32},{56,40},{64,48},{72,56},{80,... | collective-permute-start | bytes 589832 | tf_op jit(solution)/shard_map/ppermute | solution.py:26
  364.8 31.0 %collective-permute-start.4 = (bf16[1,256,768]{2,1,0:T(8,128)(2,1)}, bf16[1,256,768]{2,1,0:T(8,128)(2,1)S(1)}, u32[]{:S(2)}, u32[]{:S(2)}) collective-permute-start(bf16[1,256,768]{2,1,0:T(8,128)(2,1)} %fusion.5), channel_id=1, source_target_pairs={{7,0},{0,1},{1,2},{2,3},{3,4},{4,5},{5,6},{6,7},{15,8},{8,9},{9,10... | collective-permute-start | bytes 1179656 | tf_op jit(solution)/shard_map/ppermute | solution.py:32
  374.0 11.3 %collective-permute-start.12 = (bf16[1,128,384]{2,1,0:T(8,128)(2,1)S(1)}, bf16[1,128,384]{2,1,0:T(8,128)(2,1)S(1)}, u32[]{:S(2)}, u32[]{:S(2)}) collective-permute-start(bf16[1,128,384]{2,1,0:T(8,128)(2,1)S(1)} %get-tuple-element.15), channel_id=1, source_target_pairs={{0,8},{8,16},{16,24},{24,32},{32,40},{40,48},{48,56},{56,64},{64,7... | collective-permute-start | bytes 294920 | tf_op jit(solution)/shard_map/ppermute | solution.py:17
  383.3 9.8 %copy-start.6 = (bf16[1,1,1,768,384]{4,1,2,0,3:T(2,128)(2,1)S(1)}, bf16[1,1,1,768,384]{4,1,2,0,3:T(2,128)(2,1)}, u32[]{:S(2)}) copy-start(bf16[1,1,1,768,384]{4,1,2,0,3:T(2,128)(2,1)} %copy-done.5) | copy-start | bytes 1769476
  383.3 9.8 %copy-start.14 = (bf16[1,256,768]{2,1,0:T(8,128)(2,1)S(1)}, bf16[1,256,768]{2,1,0:T(8,128)(2,1)}, u32[]{:S(2)}) copy-start(bf16[1,256,768]{2,1,0:T(8,128)(2,1)} %param.6) | copy-start | bytes 1179652
  383.3 9.8 %collective-permute-start.11 = (bf16[1,128,384]{2,1,0:T(8,128)(2,1)S(1)}, bf16[1,128,384]{2,1,0:T(8,128)(2,1)S(1)}, u32[]{:S(2)}, u32[]{:S(2)}) collective-permute-start(bf16[1,128,384]{2,1,0:T(8,128)(2,1)S(1)} %get-tuple-element.14), channel_id=1, source_target_pairs={{8,0},{16,8},{24,16},{32,24},{40,32},{48,40},{56,48},{64,56},{72,6... | collective-permute-start | bytes 294920 | tf_op jit(solution)/shard_map/ppermute | solution.py:18
  393.9 9.4 %collective-permute-start.13 = (bf16[1,256,768]{2,1,0:T(8,128)(2,1)S(1)}, bf16[1,256,768]{2,1,0:T(8,128)(2,1)S(1)}, u32[]{:S(2)}, u32[]{:S(2)}) collective-permute-start(bf16[1,256,768]{2,1,0:T(8,128)(2,1)S(1)} %fusion.28), channel_id=1, source_target_pairs={{1,0},{2,1},{3,2},{4,3},{5,4},{6,5},{7,6},{0,7},{9,8},{10,9},{11,1... | collective-permute-start | bytes 1179656 | tf_op jit(solution)/shard_map/ppermute | solution.py:32
  (13 other events, 33.7 us)
Sparse Core Ops, SparseCore 0:
  11.2 143.1 all-gather.4
  157.7 143.1 all-gather.2
where the time goes:
time: 413 us; the launch traced here: 412 us
  waiting for transfers between devices  287 us (69%)
  starting transfers between devices  57.1 us (14%)
  matrix products  30 us (7%)
  local copies, waits for them, and re-layouts  21.2 us (5%)
  between operations  14.5 us (4%)
    all_gather x1, waiting for transfers between devices, local(): lax.all_gather(conv_weight, 'seq', axis=3, tiled=True)  141 us
    all_gather x1, waiting for transfers between devices, local(): lax.all_gather(proj_weight, 'seq', axis=2, tiled=True)  124 us
    ppermute x6, starting transfers between devices, from_behind(): return lax.ppermute(block, axis, route)  23.6 us
    ppermute x3, starting transfers between devices, padded(): before = lax.ppermute(last, axis, up)  22.2 us
    dot_general x10, matrix products, conv_apply(): jnp.einsum('krc,ch->krh', values, weight, preferred_element_type=jnp.floa...  13.1 us
    slice x1, local copies, waits for them, and re-layouts, run_forward(): middle = conv_apply(activated, conv_part[1])  9.01 us
    dot_general x3, matrix products, run_forward(): jnp.einsum('krh,hc->krc', hidden, proj_part, preferred_element_type=jnp.f...  8.49 us
  transfers between devices with their start and end apart: 16, of which 6 were waited for; matrix products, arithmetic and copies ran while one was open for 12% of the time, Pallas kernels for 0%

commit v1 on v0

--- a/solution.py
+++ b/solution.py
@@ -82,7 +82,9 @@
 def local(fwd_input, bwd_input, bwd_cotangent, conv_weight, proj_weight):
     convolution_complete, proj_full = (
         lax.all_gather(conv_weight, "seq", axis=3, tiled=True),
-        lax.all_gather(proj_weight, "seq", axis=2, tiled=True),
+        jnp.concatenate(
+            lax.all_to_all(jnp.stack([proj_weight] * lax.axis_size("seq")), "seq", 0, 0), axis=2
+        ),
     )
     pieces = [
         (convolution_complete[0, depth_level], proj_full[0, depth_level])

time: 413 us -> 281 us (0.68)
  waiting for transfers between devices: 287 us -> 141 us
  starting transfers between devices: 57.1 us -> 73.2 us
    all_gather x1 -> x0, waiting for transfers between devices: 124 us -> none  [local(): lax.all_gather(proj_weight, 'seq', axis=2, tiled=True)]
    all_gather x1, waiting for transfers between devices: 141 us -> 75 us  [local(): lax.all_gather(conv_weight, 'seq', axis=3, tiled=True)]
    all_to_all x0 -> x1, waiting for transfers between devices: none -> 44.6 us  [local(): lax.all_to_all(jnp.stack([proj_weight] * lax.axis_size('seq')), 'seq', 0, 0)]
    all_to_all x0 -> x1, starting transfers between devices: none -> 17.7 us  [local(): lax.all_to_all(jnp.stack([proj_weight] * lax.axis_size('seq')), 'seq', 0, 0)]
  transfers between devices with their start and end apart: 16 -> 16, of which waited for: 6 -> 6; matrix products, arithmetic and copies ran while one was open for 12% -> 17% of each run, Pallas kernels for 0% -> 0%
where the time goes in v1:
time: 281 us; the launch traced here: 280 us
  waiting for transfers between devices  141 us (50%)
  starting transfers between devices  73.2 us (26%)
  matrix products  30 us (11%)
  local copies, waits for them, and re-layouts  20.8 us (7%)
  between operations  14.5 us (5%)
    all_gather x1, waiting for transfers between devices, local(): lax.all_gather(conv_weight, 'seq', axis=3, tiled=True)  75 us
    all_to_all x1, waiting for transfers between devices, local(): lax.all_to_all(jnp.stack([proj_weight] * lax.axis_size('seq')), 'seq', 0, 0)  44.6 us
    ppermute x6, starting transfers between devices, from_behind(): return lax.ppermute(block, axis, route)  23.6 us
    ppermute x3, starting transfers between devices, padded(): before = lax.ppermute(last, axis, up)  20.7 us
    all_to_all x1, starting transfers between devices, local(): lax.all_to_all(jnp.stack([proj_weight] * lax.axis_size('seq')), 'seq', 0, 0)  17.7 us
    dot_general x10, matrix products, conv_apply(): jnp.einsum('krc,ch->krh', values, weight, preferred_element_type=jnp.floa...  13.1 us
    slice x1, local copies, waits for them, and re-layouts, run_forward(): middle = conv_apply(activated, conv_part[1])  9.01 us
    dot_general x3, matrix products, run_forward(): jnp.einsum('krh,hc->krc', hidden, proj_part, preferred_element_type=jnp.f...  8.48 us
  transfers between devices with their start and end apart: 16, of which 6 were waited for; matrix products, arithmetic and copies ran while one was open for 17% of the time, Pallas kernels for 0%

profile of v1, /device:TPU:103, one launch (start us, length us, event | category | flops | bytes accessed | tf_op | source)
XLA Modules:
  0.0 279.9 jit_solution(12431089959340973314)
XLA Ops:
  8.7 2.3 stack.2
  11.1 17.7 %all-to-all-start = ((bf16[64,1,2,6,768]{4,2,3,1,0:T(2,128)(2,1)}), bf16[64,1,2,6,768]{4,2,3,1,0:T(2,128)(2,1)S(1)}, u32[]{:S(2)}, u32[]{:S(2)}) async-start(bf16[64,1,2,6,768]{4,2,3,1,0:T(2,128)(2,1)} %stack.2), calls=%async_computation | async-start | bytes 2359296 | tf_op jit(solution)/shard_map/all_to_all | solution.py:86
  29.9 4.6 %collective-permute-start.5 = (bf16[1,128,768]{2,1,0:T(8,128)(2,1)}, bf16[1,128,768]{2,1,0:T(8,128)(2,1)}, u32[]{:S(2)}, u32[]{:S(2)}) collective-permute-start(bf16[1,128,768]{2,1,0:T(8,128)(2,1)} %get-tuple-element.10), channel_id=1, source_target_pairs={{0,8},{8,16},{16,24},{24,32},{32,40},{40,48},{48,56},{56,64},{64,7... | collective-permute-start | bytes 589832 | tf_op jit(solution)/shard_map/ppermute | solution.py:17
  34.5 1.9 collective-permute-start.6
  37.6 7.2 %collective-permute-start = (bf16[1,128,768]{2,1,0:T(8,128)(2,1)}, bf16[1,128,768]{2,1,0:T(8,128)(2,1)}, u32[]{:S(2)}, u32[]{:S(2)}) collective-permute-start(bf16[1,128,768]{2,1,0:T(8,128)(2,1)} %get-tuple-element.12), channel_id=1, source_target_pairs={{0,8},{8,16},{16,24},{24,32},{32,40},{40,48},{48,56},{56,64},{64,7... | collective-permute-start | bytes 589832 | tf_op jit(solution)/shard_map/ppermute | solution.py:17
  46.8 44.6 %all-to-all-done = bf16[64,1,2,6,768]{4,2,3,1,0:T(2,128)(2,1)S(1)} async-done(((bf16[64,1,2,6,768]{4,2,3,1,0:T(2,128)(2,1)}), bf16[64,1,2,6,768]{4,2,3,1,0:T(2,128)(2,1)S(1)}, u32[]{:S(2)}, u32[]{:S(2)}) %all-to-all-start) | async-done | bytes 1179680 | tf_op jit(solution)/shard_map/all_to_all | solution.py:86
  91.4 3.0 %fusion.186 = (bf16[1,1,384,768]{3,1,2,0:T(2,128)(2,1)}, bf16[1,1,384,768]{3,1,2,0:T(2,128)(2,1)}) fusion(bf16[1,2,384,768]{3,1,2,0:T(2,128)(2,1)S(1)} %bitcast.233), kind=kLoop, calls=%fused_computation.223 | loop fusion | bytes 2359296 | tf_op jit(solution)/shard_map/slice | solution.py:90
  94.4 75.0 %all-gather.2.cloned.1.call-done = bf16[1,2,3,768,384]{4,1,2,0,3:T(2,128)(2,1)} async-done(((bf16[1,2,3,12,384]{4,1,2,0,3:T(2,128)(2,1)}), bf16[1,2,3,768,384]{4,1,2,0,3:T(2,128)(2,1)}) %all-gather.2.cloned.1.call-update) | async-done | bytes 3538960 | tf_op jit(solution)/shard_map/all_gather | solution.py:84
  169.3 9.0 %fusion.185 = (bf16[1,1,1,768,384]{4,1,2,0,3:T(2,128)(2,1)}, bf16[1,1,1,768,384]{4,1,2,0,3:T(2,128)(2,1)}, bf16[1,1,1,768,384]{4,1,2,0,3:T(2,128)(2,1)S(1)}, bf1...) fusion(bf16[1,2,3,768,384]{4,1,2,0,3:T(2,128)(2,1)} %all-gather, ...), kind=kLoop, calls=%fused_computation.222 | loop fusion | bytes 7077888 | tf_op jit(solution)/shard_map/slice | solution.py:68
  184.0 3.8 %collective-permute-start.7 = (bf16[1,256,768]{2,1,0:T(8,128)(2,1)}, bf16[1,256,768]{2,1,0:T(8,128)(2,1)}, u32[]{:S(2)}, u32[]{:S(2)}) collective-permute-start(bf16[1,256,768]{2,1,0:T(8,128)(2,1)} %get-tuple-element.18), channel_id=1, source_target_pairs={{0,16},{8,24},{16,32},{24,40},{32,48},{40,56},{48,64},{56,72},{64,... | collective-permute-start | bytes 1179656 | tf_op jit(solution)/shard_map/ppermute | solution.py:26
  187.8 3.0 %collective-permute-start.8 = (bf16[1,256,768]{2,1,0:T(8,128)(2,1)}, bf16[1,256,768]{2,1,0:T(8,128)(2,1)}, u32[]{:S(2)}, u32[]{:S(2)}) collective-permute-start(bf16[1,256,768]{2,1,0:T(8,128)(2,1)} %get-tuple-element.18), channel_id=1, source_target_pairs={{16,0},{24,8},{32,16},{40,24},{48,32},{56,40},{64,48},{72,56},{80,... | collective-permute-start | bytes 1179656 | tf_op jit(solution)/shard_map/ppermute | solution.py:26
  190.8 2.0 fusion.15
  192.8 2.0 fusion.16
  194.8 3.5 %fusion.44 = (bf16[1,256,768]{2,1,0:T(8,128)(2,1)}, bf16[1,256,768]{2,1,0:T(8,128)(2,1)}) fusion(bf16[1,1,384,768]{3,1,2,0:T(2,128)(2,1)} %get-tuple-element.9, bf16[1,256,384]{2,1,0:T(8,128)(2,1)} %fusion.16, bf16[1,256,384]{2,1,0:T(8,128)(2,1)} %fusion.15, bf16[1,1,1,768,384]{4,1,2,0,3:T(2,128)(2,1)S(1)} %get-tuple-element.5, bf16[1,256,768]{2,1,0:T(8,128)(2,1)} %param.5), kind=kOutput, calls=%fused_computation.84 | convolution fusion | flops 307789824 | bytes 2752512 | tf_op jit(solution)/shard_map/krh,hc->krc/dot_general | solution.py:77
  198.3 5.9 %collective-permute-start.2 = (bf16[1,256,768]{2,1,0:T(8,128)(2,1)}, bf16[1,256,768]{2,1,0:T(8,128)(2,1)S(1)}, u32[]{:S(2)}, u32[]{:S(2)}) collective-permute-start(bf16[1,256,768]{2,1,0:T(8,128)(2,1)} %get-tuple-element.16), channel_id=1, source_target_pairs={{0,16},{8,24},{16,32},{24,40},{32,48},{40,56},{48,64},{56,72},{64,... | collective-permute-start | bytes 1179656 | tf_op jit(solution)/shard_map/ppermute | solution.py:26
  204.2 2.1 collective-permute-start.3
  208.4 6.2 %collective-permute-done.8 = bf16[1,256,768]{2,1,0:T(8,128)(2,1)} collective-permute-done((bf16[1,256,768]{2,1,0:T(8,128)(2,1)}, bf16[1,256,768]{2,1,0:T(8,128)(2,1)}, u32[]{:S(2)}, u32[]{:S(2)}) %collective-permute-start.8) | collective-permute-done | bytes 393248 | tf_op jit(solution)/shard_map/ppermute | solution.py:26
  218.5 6.9 %collective-permute-start.10 = (bf16[1,256,384]{2,1,0:T(8,128)(2,1)}, bf16[1,256,384]{2,1,0:T(8,128)(2,1)}, u32[]{:S(2)}, u32[]{:S(2)}) collective-permute-start(bf16[1,256,384]{2,1,0:T(8,128)(2,1)} %fusion.75), channel_id=1, source_target_pairs={{0,16},{8,24},{16,32},{24,40},{32,48},{40,56},{48,64},{56,72},{64,... | collective-permute-start | bytes 589832 | tf_op jit(solution)/shard_map/ppermute | solution.py:26
  229.5 3.5 %fusion.5 = bf16[1,256,768]{2,1,0:T(8,128)(2,1)} fusion(bf16[1,256,768]{2,1,0:T(8,128)(2,1)} %get-tuple-element.17, bf16[1,256,384]{2,1,0:T(8,128)(2,1)} %fusion.18, bf16[1,256,384]{2,1,0:T(8,128)(2,1)} %fusion.17, bf16[1,1,384,768]{3,1,2,0:T(2,128)(2,1)} %get-tuple-element.8, bf16[1,1,1,768,384]{4,1,2,0,3:T(2,128)(2,1)} %get-tuple-element.2), kind=kOutput, calls=%fused_computation.31 | convolution fusion | flops 305823744 | bytes 2359296 | tf_op jit(solution)/shard_map/krh,hc->krc/dot_general | solution.py:77
  233.0 3.4 %collective-permute-start.4 = (bf16[1,256,768]{2,1,0:T(8,128)(2,1)}, bf16[1,256,768]{2,1,0:T(8,128)(2,1)S(1)}, u32[]{:S(2)}, u32[]{:S(2)}) collective-permute-start(bf16[1,256,768]{2,1,0:T(8,128)(2,1)} %fusion.5), channel_id=1, source_target_pairs={{7,0},{0,1},{1,2},{2,3},{3,4},{4,5},{5,6},{6,7},{15,8},{8,9},{9,10... | collective-permute-start | bytes 1179656 | tf_op jit(solution)/shard_map/ppermute | solution.py:32
  242.2 8.8 %collective-permute-start.12 = (bf16[1,128,384]{2,1,0:T(8,128)(2,1)S(1)}, bf16[1,128,384]{2,1,0:T(8,128)(2,1)S(1)}, u32[]{:S(2)}, u32[]{:S(2)}) collective-permute-start(bf16[1,128,384]{2,1,0:T(8,128)(2,1)S(1)} %get-tuple-element.15), channel_id=1, source_target_pairs={{0,8},{8,16},{16,24},{24,32},{32,40},{40,48},{48,56},{56,64},{64,7... | collective-permute-start | bytes 294920 | tf_op jit(solution)/shard_map/ppermute | solution.py:17
  251.5 2.1 collective-permute-start.11
  254.0 7.3 %collective-permute-done.11 = bf16[1,128,384]{2,1,0:T(8,128)(2,1)S(1)} collective-permute-done((bf16[1,128,384]{2,1,0:T(8,128)(2,1)S(1)}, bf16[1,128,384]{2,1,0:T(8,128)(2,1)S(1)}, u32[]{:S(2)}, u32[]{:S(2)}) %collective-permute-start.11) | collective-permute-done | bytes 98336 | tf_op jit(solution)/shard_map/ppermute | solution.py:18
  264.0 7.5 %collective-permute-done.13 = bf16[1,256,768]{2,1,0:T(8,128)(2,1)S(1)} collective-permute-done((bf16[1,256,768]{2,1,0:T(8,128)(2,1)S(1)}, bf16[1,256,768]{2,1,0:T(8,128)(2,1)S(1)}, u32[]{:S(2)}, u32[]{:S(2)}) %collective-permute-start.13) | collective-permute-done | bytes 393248 | tf_op jit(solution)/shard_map/ppermute | solution.py:32
  (85 shorter events, 32.0 us)
Async XLA Ops:
  7.2 162.2 %all-gather.2.cloned.1.call-start = ((), (), s32[]{:S(2)}) async-start(), calls=%async_computation.1 | async-start | bytes 3594240 | tf_op jit(solution)/shard_map/all_gather | solution.py:84
  11.1 17.7 %copy-start.13 = (bf16[1,256,768]{2,1,0:T(8,128)(2,1)S(1)}, bf16[1,256,768]{2,1,0:T(8,128)(2,1)}, u32[]{:S(2)}) copy-start(bf16[1,256,768]{2,1,0:T(8,128)(2,1)} %param.6) | copy-start | bytes 1179652
  11.1 80.3 %all-to-all-start = ((bf16[64,1,2,6,768]{4,2,3,1,0:T(2,128)(2,1)}), bf16[64,1,2,6,768]{4,2,3,1,0:T(2,128)(2,1)S(1)}, u32[]{:S(2)}, u32[]{:S(2)}) async-start(bf16[64,1,2,6,768]{4,2,3,1,0:T(2,128)(2,1)} %stack.2), calls=%async_computation | async-start | bytes 2359296 | tf_op jit(solution)/shard_map/all_to_all | solution.py:86
  29.9 148.5 %collective-permute-start.5 = (bf16[1,128,768]{2,1,0:T(8,128)(2,1)}, bf16[1,128,768]{2,1,0:T(8,128)(2,1)}, u32[]{:S(2)}, u32[]{:S(2)}) collective-permute-start(bf16[1,128,768]{2,1,0:T(8,128)(2,1)} %get-tuple-element.10), channel_id=1, source_target_pairs={{0,8},{8,16},{16,24},{24,32},{32,40},{40,48},{48,56},{56,64},{64,7... | collective-permute-start | bytes 589832 | tf_op jit(solution)/shard_map/ppermute | solution.py:17
  34.5 145.4 %collective-permute-start.6 = (bf16[1,128,768]{2,1,0:T(8,128)(2,1)}, bf16[1,128,768]{2,1,0:T(8,128)(2,1)}, u32[]{:S(2)}, u32[]{:S(2)}) collective-permute-start(bf16[1,128,768]{2,1,0:T(8,128)(2,1)} %get-tuple-element.11), channel_id=1, source_target_pairs={{8,0},{16,8},{24,16},{32,24},{40,32},{48,40},{56,48},{64,56},{72,6... | collective-permute-start | bytes 589832 | tf_op jit(solution)/shard_map/ppermute | solution.py:18
  36.7 57.7 %copy-start.1 = (bf16[1,256,768]{2,1,0:T(8,128)(2,1)}, bf16[1,256,768]{2,1,0:T(8,128)(2,1)S(1)}, u32[]{:S(2)}) copy-start(bf16[1,256,768]{2,1,0:T(8,128)(2,1)S(1)} %fusion.38) | copy-start | bytes 1179652
  37.6 153.2 %collective-permute-start = (bf16[1,128,768]{2,1,0:T(8,128)(2,1)}, bf16[1,128,768]{2,1,0:T(8,128)(2,1)}, u32[]{:S(2)}, u32[]{:S(2)}) collective-permute-start(bf16[1,128,768]{2,1,0:T(8,128)(2,1)} %get-tuple-element.12), channel_id=1, source_target_pairs={{0,8},{8,16},{16,24},{24,32},{32,40},{40,48},{48,56},{56,64},{64,7... | collective-permute-start | bytes 589832 | tf_op jit(solution)/shard_map/ppermute | solution.py:17
  44.8 148.0 %collective-permute-start.1 = (bf16[1,128,768]{2,1,0:T(8,128)(2,1)}, bf16[1,128,768]{2,1,0:T(8,128)(2,1)}, u32[]{:S(2)}, u32[]{:S(2)}) collective-permute-start(bf16[1,128,768]{2,1,0:T(8,128)(2,1)} %get-tuple-element.13), channel_id=1, source_target_pairs={{8,0},{16,8},{24,16},{32,24},{40,32},{48,40},{56,48},{64,56},{72,6... | collective-permute-start | bytes 589832 | tf_op jit(solution)/shard_map/ppermute | solution.py:18
  178.4 12.5 %copy-start.5 = (bf16[1,1,1,768,384]{4,1,2,0,3:T(2,128)(2,1)}, bf16[1,1,1,768,384]{4,1,2,0,3:T(2,128)(2,1)S(1)}, u32[]{:S(2)}) copy-start(bf16[1,1,1,768,384]{4,1,2,0,3:T(2,128)(2,1)S(1)} %get-tuple-element.6) | copy-start | bytes 1769476
  184.0 22.5 %collective-permute-start.7 = (bf16[1,256,768]{2,1,0:T(8,128)(2,1)}, bf16[1,256,768]{2,1,0:T(8,128)(2,1)}, u32[]{:S(2)}, u32[]{:S(2)}) collective-permute-start(bf16[1,256,768]{2,1,0:T(8,128)(2,1)} %get-tuple-element.18), channel_id=1, source_target_pairs={{0,16},{8,24},{16,32},{24,40},{32,48},{40,56},{48,64},{56,72},{64,... | collective-permute-start | bytes 1179656 | tf_op jit(solution)/shard_map/ppermute | solution.py:26
  187.8 26.8 %collective-permute-start.8 = (bf16[1,256,768]{2,1,0:T(8,128)(2,1)}, bf16[1,256,768]{2,1,0:T(8,128)(2,1)}, u32[]{:S(2)}, u32[]{:S(2)}) collective-permute-start(bf16[1,256,768]{2,1,0:T(8,128)(2,1)} %get-tuple-element.18), channel_id=1, source_target_pairs={{16,0},{24,8},{32,16},{40,24},{48,32},{56,40},{64,48},{72,56},{80,... | collective-permute-start | bytes 1179656 | tf_op jit(solution)/shard_map/ppermute | solution.py:26
  198.3 29.1 %collective-permute-start.2 = (bf16[1,256,768]{2,1,0:T(8,128)(2,1)}, bf16[1,256,768]{2,1,0:T(8,128)(2,1)S(1)}, u32[]{:S(2)}, u32[]{:S(2)}) collective-permute-start(bf16[1,256,768]{2,1,0:T(8,128)(2,1)} %get-tuple-element.16), channel_id=1, source_target_pairs={{0,16},{8,24},{16,32},{24,40},{32,48},{40,56},{48,64},{56,72},{64,... | collective-permute-start | bytes 1179656 | tf_op jit(solution)/shard_map/ppermute | solution.py:26
  204.2 24.2 %collective-permute-start.3 = (bf16[1,256,768]{2,1,0:T(8,128)(2,1)}, bf16[1,256,768]{2,1,0:T(8,128)(2,1)S(1)}, u32[]{:S(2)}, u32[]{:S(2)}) collective-permute-start(bf16[1,256,768]{2,1,0:T(8,128)(2,1)} %get-tuple-element.16), channel_id=1, source_target_pairs={{16,0},{24,8},{32,16},{40,24},{48,32},{56,40},{64,48},{72,56},{80,... | collective-permute-start | bytes 1179656 | tf_op jit(solution)/shard_map/ppermute | solution.py:26
  206.5 9.4 %copy-start = (bf16[1,1,1,768,384]{4,1,2,0,3:T(2,128)(2,1)S(1)}, bf16[1,1,1,768,384]{4,1,2,0,3:T(2,128)(2,1)}, u32[]{:S(2)}) copy-start(bf16[1,1,1,768,384]{4,1,2,0,3:T(2,128)(2,1)} %get-tuple-element.2) | copy-start | bytes 1769476
  206.5 9.4 %copy-start.20 = (bf16[1,256,768]{2,1,0:T(8,128)(2,1)S(1)}, bf16[1,256,768]{2,1,0:T(8,128)(2,1)}, u32[]{:S(2)}) copy-start(bf16[1,256,768]{2,1,0:T(8,128)(2,1)} %get-tuple-element.19) | copy-start | bytes 1179652
  217.3 10.1 %copy-start.7 = (bf16[1,1,1,768,384]{4,1,2,0,3:T(2,128)(2,1)S(1)}, bf16[1,1,1,768,384]{4,1,2,0,3:T(2,128)(2,1)}, u32[]{:S(2)}) copy-start(bf16[1,1,1,768,384]{4,1,2,0,3:T(2,128)(2,1)} %get-tuple-element.3) | copy-start | bytes 1769476
  218.5 19.8 %collective-permute-start.10 = (bf16[1,256,384]{2,1,0:T(8,128)(2,1)}, bf16[1,256,384]{2,1,0:T(8,128)(2,1)}, u32[]{:S(2)}, u32[]{:S(2)}) collective-permute-start(bf16[1,256,384]{2,1,0:T(8,128)(2,1)} %fusion.75), channel_id=1, source_target_pairs={{0,16},{8,24},{16,32},{24,40},{32,48},{40,56},{48,64},{56,72},{64,... | collective-permute-start | bytes 589832 | tf_op jit(solution)/shard_map/ppermute | solution.py:26
  225.5 14.3 %collective-permute-start.9 = (bf16[1,256,384]{2,1,0:T(8,128)(2,1)}, bf16[1,256,384]{2,1,0:T(8,128)(2,1)}, u32[]{:S(2)}, u32[]{:S(2)}) collective-permute-start(bf16[1,256,384]{2,1,0:T(8,128)(2,1)} %fusion.75), channel_id=1, source_target_pairs={{16,0},{24,8},{32,16},{40,24},{48,32},{56,40},{64,48},{72,56},{80,... | collective-permute-start | bytes 589832 | tf_op jit(solution)/shard_map/ppermute | solution.py:26
  233.0 31.0 %collective-permute-start.4 = (bf16[1,256,768]{2,1,0:T(8,128)(2,1)}, bf16[1,256,768]{2,1,0:T(8,128)(2,1)S(1)}, u32[]{:S(2)}, u32[]{:S(2)}) collective-permute-start(bf16[1,256,768]{2,1,0:T(8,128)(2,1)} %fusion.5), channel_id=1, source_target_pairs={{7,0},{0,1},{1,2},{2,3},{3,4},{4,5},{5,6},{6,7},{15,8},{8,9},{9,10... | collective-permute-start | bytes 1179656 | tf_op jit(solution)/shard_map/ppermute | solution.py:32
  242.2 11.3 %collective-permute-start.12 = (bf16[1,128,384]{2,1,0:T(8,128)(2,1)S(1)}, bf16[1,128,384]{2,1,0:T(8,128)(2,1)S(1)}, u32[]{:S(2)}, u32[]{:S(2)}) collective-permute-start(bf16[1,128,384]{2,1,0:T(8,128)(2,1)S(1)} %get-tuple-element.15), channel_id=1, source_target_pairs={{0,8},{8,16},{16,24},{24,32},{32,40},{40,48},{48,56},{56,64},{64,7... | collective-permute-start | bytes 294920 | tf_op jit(solution)/shard_map/ppermute | solution.py:17
  251.5 9.8 %copy-start.6 = (bf16[1,1,1,768,384]{4,1,2,0,3:T(2,128)(2,1)S(1)}, bf16[1,1,1,768,384]{4,1,2,0,3:T(2,128)(2,1)}, u32[]{:S(2)}) copy-start(bf16[1,1,1,768,384]{4,1,2,0,3:T(2,128)(2,1)} %copy-done.5) | copy-start | bytes 1769476
  251.5 9.8 %copy-start.15 = (bf16[1,256,768]{2,1,0:T(8,128)(2,1)S(1)}, bf16[1,256,768]{2,1,0:T(8,128)(2,1)}, u32[]{:S(2)}) copy-start(bf16[1,256,768]{2,1,0:T(8,128)(2,1)} %param.6) | copy-start | bytes 1179652
  251.5 9.8 %collective-permute-start.11 = (bf16[1,128,384]{2,1,0:T(8,128)(2,1)S(1)}, bf16[1,128,384]{2,1,0:T(8,128)(2,1)S(1)}, u32[]{:S(2)}, u32[]{:S(2)}) collective-permute-start(bf16[1,128,384]{2,1,0:T(8,128)(2,1)S(1)} %get-tuple-element.14), channel_id=1, source_target_pairs={{8,0},{16,8},{24,16},{32,24},{40,32},{48,40},{56,48},{64,56},{72,6... | collective-permute-start | bytes 294920 | tf_op jit(solution)/shard_map/ppermute | solution.py:18
  262.1 9.4 %collective-permute-start.13 = (bf16[1,256,768]{2,1,0:T(8,128)(2,1)S(1)}, bf16[1,256,768]{2,1,0:T(8,128)(2,1)S(1)}, u32[]{:S(2)}, u32[]{:S(2)}) collective-permute-start(bf16[1,256,768]{2,1,0:T(8,128)(2,1)S(1)} %fusion.28), channel_id=1, source_target_pairs={{1,0},{2,1},{3,2},{4,3},{5,4},{6,5},{7,6},{0,7},{9,8},{10,9},{11,1... | collective-permute-start | bytes 1179656 | tf_op jit(solution)/shard_map/ppermute | solution.py:32
  (14 other events, 48.1 us)
Sparse Core Ops, SparseCore 0:
  11.3 158.0 all-gather.1
